TPU v7x, 256 devices: a whole 4x4x8 slice. The times are simulated.
256 devices in a mesh: row: 8 (over y, core), col: 8 (over z_hi, x), page: 4 (over z_lo).
Axes of the slice: x: 4, y: 4, z: 8 (z_hi: 2, z_lo: 4; z = z_hi * 4 + z_lo), core: 2. Of those that a mesh axis runs over, the one named last changes fastest.
Arguments:
- tokens: bfloat16 [32, 512, 2048], P(('row', 'page'), None, 'col'), may hold values from -6 to 6
- lengths: int32 [32], P(('row', 'page')), may hold values from 1 to 512, 4096 in all
- page_slot: int32 [32, 4], P('row'), may hold values from 0 to 15, as said below
- w_query: float32 [2048, 1024], P(('row', 'page'), 'col'), may hold values from -0.125 to 0.125
- w_keyval: float32 [2, 2048, 256], P(None, ('row', 'page')), may hold values from -0.125 to 0.125
- w_out: float32 [1024, 2048], P('col', ('row', 'page')), may hold values from -0.1875 to 0.1875
- w_gateup: float32 [2, 2048, 5120], P(None, ('row', 'page'), 'col'), may hold values from -0.125 to 0.125
- w_down: float32 [5120, 2048], P('col', ('row', 'page')), may hold values from -0.078125 to 0.078125
- attn_gain: float32 [2048], replicated, may hold values from 0.1 to 1.9
- ffn_gain: float32 [2048], replicated, may hold values from 0.1 to 1.9
- query_gain: float32 [64], replicated, may hold values from 0.1 to 1.9
- key_gain: float32 [64], replicated, may hold values from 0.1 to 1.9
Outputs:
- layer_out: bfloat16 [32, 512, 2048], P(('row', 'page'), None, 'col')
- kv_pages: bfloat16 [2, 128, 128, 1024], P(None, ('row', 'page'), None, 'col')
Inputs may be any that keep to these rules, and one draw needn't show every extreme that they name: `lengths`: each prompt's real tokens; in every draw some prompt has exactly 512. `page_slot`: within the prompts of one index of row the values are a permutation; page v belongs to index v // 4 of page; the 4 blocks of the prompts of one device send the same number of blocks to each of the 4 indices of page.
All inputs are finite; a program needn't handle non-finite values. No bound on the sum of `lengths` on one device may be relied on, other than what follows from the above.
Results may differ from a plain program's by a relative error of at most 0.012.
Values may be sent and summed in bfloat16 or wider, within the bound.
No kernel may reach another device: no remote copies, remote signals or barrier semaphores. Data moves between devices by JAX's collectives and lax.ppermute only.
A program may use at most 64 MiB of HBM per device.

v0:
```python
import jax
import jax.numpy as jnp
from jax import lax
from jax.sharding import PartitionSpec as P

PAGE_LEN = 128


def normalize(values, norm_gain):
    mean_sq = jnp.mean(values * values, axis=-1, keepdims=True)
    return values * lax.rsqrt(mean_sq + 1e-06) * norm_gain


def rotate(values):
    row_count = values.shape[-3]
    head_dim = values.shape[-1]
    half_dim = head_dim // 2
    frequency = 10000.0 ** (-2.0 * jnp.arange(half_dim, dtype=jnp.float32) / head_dim)
    angles = jnp.arange(row_count, dtype=jnp.float32)[:, None] * frequency[None, :]
    cosine = jnp.cos(angles)[:, None, :]
    sine_table = jnp.sin(angles)[:, None, :]
    leading = values[..., :half_dim]
    trailing = values[..., half_dim:]
    return jnp.concatenate(
        [leading * cosine - trailing * sine_table, trailing * cosine + leading * sine_table],
        axis=-1,
    )


def attend(query_rows, key_rows, value_rows, length):
    row_count = query_rows.shape[0]
    scores = jnp.einsum(
        "qhd,khd->hqk", query_rows, key_rows, preferred_element_type=jnp.float32
    ) * query_rows.shape[2] ** (-0.5)
    positions = jnp.arange(row_count, dtype=jnp.int32)
    seen_keys = (positions[None, :] <= positions[:, None]) & (positions[None, :] < length)
    exp_scores = jnp.where(seen_keys[None], jnp.exp(scores), 0.0)
    attn_probs = (exp_scores / jnp.sum(exp_scores, axis=-1, keepdims=True)).astype(jnp.bfloat16)
    attended = jnp.einsum(
        "hqk,khd->qhd", attn_probs, value_rows, preferred_element_type=jnp.float32
    )
    live_rows = (positions < length)[:, None, None]
    return jnp.where(live_rows, attended, 0.0).astype(jnp.bfloat16)


def contract_rows(lhs, rhs_t):
    return lax.dot_general(lhs, rhs_t, (((1,), (1,)), ((), ())), preferred_element_type=jnp.float32)


def on_device(
    tokens,
    lengths,
    page_slot,
    w_query,
    w_keyval,
    w_out,
    w_gateup,
    w_down,
    attn_gain,
    ffn_gain,
    query_gain,
    key_gain,
):
    col_count = lax.axis_size("col")
    col_index = lax.axis_index("col")
    head_dim = query_gain.shape[0]
    local_width = w_query.shape[1]
    local_heads = local_width // head_dim
    kv_heads = w_keyval.shape[2] // head_dim
    group_size = local_heads * col_count // kv_heads
    assert group_size % local_heads == 0
    kv_head = col_index * local_heads // group_size
    unit_count = w_gateup.shape[2]
    kv_piece = lax.dynamic_slice_in_dim(w_keyval, kv_head * head_dim, head_dim, axis=2)
    pieces = [
        w_query.astype(jnp.bfloat16),
        jnp.transpose(kv_piece.astype(jnp.bfloat16), (1, 0, 2)).reshape(kv_piece.shape[1], -1),
        jnp.transpose(w_out.astype(jnp.bfloat16)),
        jnp.transpose(w_gateup.astype(jnp.bfloat16), (1, 0, 2)).reshape(w_gateup.shape[1], -1),
        jnp.transpose(w_down.astype(jnp.bfloat16)),
    ]
    widths = [p.shape[1] for p in pieces]
    packed = jnp.concatenate(pieces, axis=1)
    full = lax.all_gather(packed, ("row", "page"), axis=0, tiled=True)
    offsets = [sum(widths[:i]) for i in range(len(widths) + 1)]
    qkv_w = full[:, offsets[0] : offsets[2]]
    out_t = full[:, offsets[2] : offsets[3]]
    gateup_w = full[:, offsets[3] : offsets[4]]
    down_t = full[:, offsets[4] : offsets[5]]
    prompt_count, seq_len, local_feat = tokens.shape
    gathered = lax.all_gather(tokens, "col", axis=2, tiled=True)
    model_width = gathered.shape[2]
    attn_in = normalize(gathered.astype(jnp.float32), attn_gain).astype(jnp.bfloat16)
    projected = jnp.dot(attn_in.reshape(-1, model_width), qkv_w, preferred_element_type=jnp.float32)
    projected = projected.reshape(prompt_count, seq_len, local_heads + 2, head_dim)
    queries = rotate(normalize(projected[:, :, :local_heads], query_gain)).astype(jnp.bfloat16)
    keys_one = rotate(normalize(projected[:, :, local_heads : local_heads + 1], key_gain)).astype(
        jnp.bfloat16
    )
    values_one = projected[:, :, local_heads + 1 : local_heads + 2].astype(jnp.bfloat16)
    keys_rot = jnp.broadcast_to(keys_one, queries.shape)
    values_in = jnp.broadcast_to(values_one, queries.shape)
    attended = jnp.stack(
        [
            attend(queries[i], keys_rot[i], values_in[i], lengths[i]).reshape(seq_len, local_width)
            for i in range(prompt_count)
        ]
    )
    attn_terms = contract_rows(attended.reshape(-1, local_width), out_t)
    attn_terms = attn_terms.reshape(prompt_count, seq_len, model_width).astype(jnp.bfloat16)
    attn_sum = lax.psum(attn_terms, "col").astype(jnp.float32)
    residual_all = (gathered.astype(jnp.float32) + attn_sum).astype(jnp.bfloat16)
    residual = lax.dynamic_slice_in_dim(residual_all, col_index * local_feat, local_feat, axis=2)
    ffn_in = normalize(residual_all.astype(jnp.float32), ffn_gain).astype(jnp.bfloat16)
    gate_up = jnp.dot(ffn_in.reshape(-1, model_width), gateup_w, preferred_element_type=jnp.float32)
    hidden = (jax.nn.silu(gate_up[:, :unit_count]) * gate_up[:, unit_count:]).astype(jnp.bfloat16)
    ffn_terms = contract_rows(hidden, down_t).reshape(prompt_count, seq_len, model_width)
    ffn_sum = lax.psum_scatter(
        ffn_terms.astype(jnp.bfloat16), "col", scatter_dimension=2, tiled=True
    ).astype(jnp.float32)
    layer_out = (residual.astype(jnp.float32) + ffn_sum).astype(jnp.bfloat16)
    page_count = lax.axis_size("page")
    page_index = lax.axis_index("page")
    blocks_each = prompt_count * (seq_len // PAGE_LEN)
    capacity = blocks_each // page_count
    owners = page_slot // blocks_each
    local_slot = page_slot % blocks_each
    same_owner = owners[:, :, None] == owners[:, None, :]
    earlier = (
        jnp.arange(blocks_each, dtype=jnp.int32)[None, :]
        < jnp.arange(blocks_each, dtype=jnp.int32)[:, None]
    )
    order_in = jnp.sum((same_owner & earlier[None]).astype(jnp.int32), axis=2)
    my_owners = lax.dynamic_index_in_dim(owners, page_index, 0, keepdims=False)
    my_order = lax.dynamic_index_in_dim(order_in, page_index, 0, keepdims=False)
    send_pos = my_owners * capacity + my_order
    live_rows = (jnp.arange(seq_len, dtype=jnp.int32)[None, :] < lengths[:, None])[:, :, None, None]
    page_keys = jnp.where(live_rows, keys_rot, jnp.zeros_like(keys_rot)).reshape(
        blocks_each, PAGE_LEN, local_width
    )
    page_values = jnp.where(live_rows, values_in, jnp.zeros_like(values_in)).reshape(
        blocks_each, PAGE_LEN, local_width
    )
    stacked = jnp.stack([page_keys, page_values])
    outgoing = jnp.zeros_like(stacked).at[:, send_pos].set(stacked)
    incoming = lax.all_to_all(outgoing, "page", split_axis=1, concat_axis=1, tiled=True)
    arrival_hit = (owners[:, None, :] == page_index) & (
        order_in[:, None, :] == jnp.arange(capacity, dtype=jnp.int32)[None, :, None]
    )
    arrival_slot = jnp.sum(jnp.where(arrival_hit, local_slot[:, None, :], 0), axis=2).reshape(
        blocks_each
    )
    kv_pages = jnp.zeros_like(incoming).at[:, arrival_slot].set(incoming)
    return (layer_out, kv_pages)


def solution(mesh):
    in_specs = (
        P(("row", "page"), None, "col"),
        P(("row", "page")),
        P("row", None),
        P(("row", "page"), "col"),
        P(None, ("row", "page"), None),
        P("col", ("row", "page")),
        P(None, ("row", "page"), "col"),
        P("col", ("row", "page")),
        P(),
        P(),
        P(),
        P(),
    )
    out_specs = (P(("row", "page"), None, "col"), P(None, ("row", "page"), None, "col"))
    return jax.shard_map(
        on_device, mesh=mesh, in_specs=in_specs, out_specs=out_specs, check_vma=False
    )
```

profile of v0, /device:TPU:8, one launch (start us, length us, event | category | flops | bytes accessed | tf_op | source)
XLA Modules:
  0.0 443.9 jit_solution(3106016607968333589)
XLA Ops:
  8.3 1.0 convert_bitcast_fusion
  9.3 0.8 convert_dynamic-update-slice_fusion
  10.1 0.8 bitcast_dynamic-update-slice_fusion.1
  10.9 0.9 bitcast_dynamic-update-slice_fusion
  13.3 1.0 fusion.42
  14.4 74.6 %all-gather.3.cloned.1.call-done = bf16[1,512,2048]{2,1,0:T(8,128)(2,1)} async-done(((bf16[1,512,256]{2,1,0:T(8,128)(2,1)}), bf16[1,512,2048]{2,1,0:T(8,128)(2,1)}) %all-gather.3.cloned.1.call-update) | async-done | bytes 2097168 | tf_op jit(solution)/shard_map/all_gather | solution.py:91
  89.0 2.1 fusion.5
  91.0 91.8 %all-gather.5.cloned.1.call-done = bf16[2048,2304]{1,0:T(8,128)(2,1)} async-done(((bf16[64,2304]{1,0:T(8,128)(2,1)}), bf16[2048,2304]{1,0:T(8,128)(2,1)}) %all-gather.5.cloned.1.call-update) | async-done | bytes 9437200 | tf_op jit(solution)/shard_map/all_gather | solution.py:84
  182.9 1.3 slice_bitcast_fusion
  184.2 1.4 copy.35
  185.6 2.1 fusion.23
  188.5 0.7 fusion.21
  189.9 3.2 fusion.10
  193.2 131.7 %all-reduce.2.cloned.1.call-done = bf16[1,512,2048]{2,1,0:T(8,128)(2,1)} async-done(((bf16[1,512,2048]{2,1,0:T(8,128)(2,1)}), bf16[1,512,2048]{2,1,0:T(8,128)(2,1)}) %all-reduce.2.cloned.1.call-update) | async-done | bytes 2097168 | tf_op jit(solution)/shard_map/psum | solution.py:111
  324.9 2.6 fusion.2
  327.5 6.2 %fusion = f32[512,1280]{1,0:T(8,128)S(1)} fusion(bf16[2048,2304]{1,0:T(8,128)(2,1)} %all-gather.5.cloned.1.call-done, bf16[1,512,2048]{2,1,0:T(8,128)(2,1)S(1)} %get-tuple-element.3, f32[2048]{0:T(1024)S(1)} %copy-done.10, f32[512]{0:T(512)S(1)} %add_rsqrt_fusion.1), kind=kOutput, calls=%fused_computation.7 | convolution fusion | flops 2688548864 | bytes 9971712 | tf_op jit(solution)/shard_map/dot_general | solution.py:115
  333.6 5.0 %fusion.9 = bf16[1,512,2048]{2,1,0:T(8,128)(2,1)} fusion(bf16[2048,2304]{1,0:T(8,128)(2,1)} %all-gather.5.cloned.1.call-done, f32[512,1280]{1,0:T(8,128)S(1)} %fusion), kind=kOutput, calls=%fused_computation.18 | convolution fusion | flops 1345191936 | bytes 7340032 | tf_op jit(solution)/shard_map/dot_general | solution.py:47
  340.3 0.8 scatter_fusion
  341.0 0.7 copy.38
  341.8 5.9 %all-to-all-start = ((bf16[2,4,128,128]{3,2,0,1:T(8,128)(2,1)}), bf16[2,4,128,128]{3,2,0,1:T(8,128)(2,1)S(1)}, u32[]{:S(2)}, u32[]{:S(2)}) async-start(bf16[2,4,128,128]{3,2,0,1:T(8,128)(2,1)} %copy.38), calls=%async_computation.1 | async-start | bytes 524288 | tf_op jit(solution)/shard_map/all_to_all | solution.py:146
  347.8 6.7 %all-to-all-done = bf16[2,4,128,128]{3,2,0,1:T(8,128)(2,1)S(1)} async-done(((bf16[2,4,128,128]{3,2,0,1:T(8,128)(2,1)}), bf16[2,4,128,128]{3,2,0,1:T(8,128)(2,1)S(1)}, u32[]{:S(2)}, u32[]{:S(2)}) %all-to-all-start) | async-done | bytes 262176 | tf_op jit(solution)/shard_map/all_to_all | solution.py:146
  354.6 0.8 scatter_fusion.1
  355.4 80.2 %reduce-scatter.2.cloned.1.call-done = bf16[1,512,256]{2,1,0:T(8,128)(2,1)} async-done(((bf16[1,512,2048]{2,1,0:T(8,128)(2,1)}), bf16[1,512,256]{2,1,0:T(8,128)(2,1)}) %reduce-scatter.2.cloned.1.call-update) | async-done | bytes 262160 | tf_op jit(solution)/shard_map/reduce_scatter | solution.py:118
  435.6 1.8 add_convert_fusion
  (68 shorter events, 5.2 us)
Async XLA Ops:
  7.2 0.9 copy-start
  7.2 81.8 %all-gather.3.cloned.1.call-start = ((), (), s32[]{:S(2)}) async-start(), calls=%async_computation.2 | async-start | bytes 2359296 | tf_op jit(solution)/shard_map/all_gather | solution.py:91
  7.9 174.9 %all-gather.5.cloned.1.call-start = ((), (), s32[]{:S(2)}) async-start(), calls=%async_computation.3 | async-start | bytes 9732096 | tf_op jit(solution)/shard_map/all_gather | solution.py:84
  11.8 0.7 copy-start.4
  12.5 312.3 %all-reduce.2.cloned.1.call-start = ((), (), s32[]{:S(2)}) async-start(), calls=%async_computation.4 | async-start | bytes 4194304 | tf_op jit(solution)/shard_map/psum | solution.py:111
  91.0 94.6 %copy-start.1 = (bf16[1,512,2048]{2,1,0:T(8,128)(2,1)S(1)}, bf16[1,512,2048]{2,1,0:T(8,128)(2,1)}, u32[]{:S(2)}) copy-start(bf16[1,512,2048]{2,1,0:T(8,128)(2,1)} %all-gather.3.cloned.1.call-done) | copy-start | bytes 6291460
  185.6 2.2 copy-start.8
  185.6 2.7 copy-start.9
  185.6 2.8 copy-start.5
  185.6 2.8 copy-start.6
  193.1 134.3 %copy-start.10 = (f32[2048]{0:T(1024)S(1)}, f32[2048]{0:T(1024)}, u32[]{:S(2)}) copy-start(f32[2048]{0:T(1024)} %param.21) | copy-start | bytes 24580
  193.2 242.5 %reduce-scatter.2.cloned.1.call-start = ((), (), s32[]{:S(2)}) async-start(), calls=%async_computation.5 | async-start | bytes 2359296 | tf_op jit(solution)/shard_map/reduce_scatter | solution.py:118
  327.4 6.2 %copy-start.2 = (bf16[1,512,2048]{2,1,0:T(8,128)(2,1)}, bf16[1,512,2048]{2,1,0:T(8,128)(2,1)S(1)}, u32[]{:S(2)}) copy-start(bf16[1,512,2048]{2,1,0:T(8,128)(2,1)S(1)} %get-tuple-element.3) | copy-start | bytes 6291460
  338.7 0.7 copy-start.7
  341.8 12.8 %all-to-all-start = ((bf16[2,4,128,128]{3,2,0,1:T(8,128)(2,1)}), bf16[2,4,128,128]{3,2,0,1:T(8,128)(2,1)S(1)}, u32[]{:S(2)}, u32[]{:S(2)}) async-start(bf16[2,4,128,128]{3,2,0,1:T(8,128)(2,1)} %copy.38), calls=%async_computation.1 | async-start | bytes 524288 | tf_op jit(solution)/shard_map/all_to_all | solution.py:146
  355.4 82.0 %copy-start.3 = (bf16[2,4,128,128]{3,2,1,0:T(8,128)(2,1)}, bf16[2,4,128,128]{3,2,1,0:T(8,128)(2,1)S(1)}, u32[]{:S(2)}) copy-start(bf16[2,4,128,128]{3,2,1,0:T(8,128)(2,1)S(1)} %scatter_fusion.1) | copy-start | bytes 786436
Sparse Core Ops, SparseCore 0:
  10.5 78.4 all-gather.2
  90.8 92.0 all-gather.4
  193.3 131.5 all-reduce.1
  338.8 96.7 reduce-scatter.1
where the time goes:
time: 445 us; the launch traced here: 444 us
  waiting for transfers between devices  386 us (87%)
  matrix products  17.9 us (4%)
  between operations  14.8 us (3%)
  other arithmetic  12.3 us (3%)
  local copies, waits for them, and re-layouts  7.11 us (2%)
  starting transfers between devices  6.08 us (1%)
    psum x1, waiting for transfers between devices, on_device(): attn_sum = lax.psum(attn_terms, 'col').astype(jnp.float32)  132 us
    all_gather x1, waiting for transfers between devices, on_device(): full = lax.all_gather(packed, ('row', 'page'), axis=0, tiled=True)  91.8 us
    reduce_scatter x1, waiting for transfers between devices, on_device(): lax.psum_scatter(ffn_terms.astype(jnp.bfloat16), 'col', scatter_dimension...  80.2 us
    all_gather x1, waiting for transfers between devices, on_device(): gathered = lax.all_gather(tokens, 'col', axis=2, tiled=True)  74.6 us
  transfers between devices with their start and end apart: 5, of which 5 were waited for; matrix products, arithmetic and copies ran while one was open for 2% of the time, Pallas kernels for 0%

commit v1 on v0

--- a/solution.py
+++ b/solution.py
@@ -81,7 +81,10 @@
     ]
     widths = [p.shape[1] for p in pieces]
     packed = jnp.concatenate(pieces, axis=1)
-    full = lax.all_gather(packed, ("row", "page"), axis=0, tiled=True)
+    full = jnp.concatenate(
+        lax.all_to_all(jnp.stack([packed] * lax.axis_size(("row", "page"))), ("row", "page"), 0, 0),
+        axis=0,
+    )
     offsets = [sum(widths[:i]) for i in range(len(widths) + 1)]
     qkv_w = full[:, offsets[0] : offsets[2]]
     out_t = full[:, offsets[2] : offsets[3]]

time: 445 us -> 520 us (1.17)
  waiting for transfers between devices: 386 us -> 447 us
  starting transfers between devices: 6.08 us -> 15.2 us
    all_to_all x0 -> x1, waiting for transfers between devices: none -> 130 us  [on_device(): lax.all_to_all(jnp.stack([packed] * lax.axis_size(('row', 'page'))), ('ro...]
    all_gather x1 -> x0, waiting for transfers between devices: 91.8 us -> none  [on_device(): full = lax.all_gather(packed, ('row', 'page'), axis=0, tiled=True)]
    all_gather x1, waiting for transfers between devices: 74.6 us -> 92.7 us  [on_device(): gathered = lax.all_gather(tokens, 'col', axis=2, tiled=True)]
    all_to_all x0 -> x1, starting transfers between devices: none -> 9.18 us  [on_device(): lax.all_to_all(jnp.stack([packed] * lax.axis_size(('row', 'page'))), ('ro...]
  transfers between devices with their start and end apart: 5 -> 5, of which waited for: 5 -> 5; matrix products, arithmetic and copies ran while one was open for 2% -> 1% of each run, Pallas kernels for 0% -> 0%
where the time goes in v1:
time: 520 us; the launch traced here: 519 us
  waiting for transfers between devices  447 us (86%)
  matrix products  17.9 us (3%)
  starting transfers between devices  15.2 us (3%)
  between operations  14.7 us (3%)
  other arithmetic  12.3 us (2%)
  local copies, waits for them, and re-layouts  12 us (2%)
    psum x1, waiting for transfers between devices, on_device(): attn_sum = lax.psum(attn_terms, 'col').astype(jnp.float32)  137 us
    all_to_all x1, waiting for transfers between devices, on_device(): lax.all_to_all(jnp.stack([packed] * lax.axis_size(('row', 'page'))), ('ro...  130 us
    all_gather x1, waiting for transfers between devices, on_device(): gathered = lax.all_gather(tokens, 'col', axis=2, tiled=True)  92.7 us
    reduce_scatter x1, waiting for transfers between devices, on_device(): lax.psum_scatter(ffn_terms.astype(jnp.bfloat16), 'col', scatter_dimension...  80.5 us
  transfers between devices with their start and end apart: 5, of which 5 were waited for; matrix products, arithmetic and copies ran while one was open for 1% of the time, Pallas kernels for 0%

profile of v1, /device:TPU:8, one launch (start us, length us, event | category | flops | bytes accessed | tf_op | source)
XLA Modules:
  0.0 519.1 jit_solution(15339647319856996533)
XLA Ops:
  7.2 0.9 copy-done
  9.1 1.0 convert_bitcast_fusion
  10.1 0.8 bitcast_dynamic-update-slice_fusion.1
  10.9 0.9 bitcast_dynamic-update-slice_fusion
  11.8 4.7 stack.4
  16.5 9.2 %all-to-all-start = ((bf16[32,64,2304]{2,1,0:T(8,128)(2,1)}), bf16[32,64,2304]{2,1,0:T(8,128)(2,1)}, u32[]{:S(2)}, u32[]{:S(2)}) async-start(bf16[32,64,2304]{2,1,0:T(8,128)(2,1)} %stack.4), calls=%async_computation | async-start | bytes 18874368 | tf_op jit(solution)/shard_map/all_to_all | solution.py:85
  27.2 1.0 fusion.42
  28.3 92.7 %all-gather.2.cloned.1.call-done = bf16[1,512,2048]{2,1,0:T(8,128)(2,1)} async-done(((bf16[1,512,256]{2,1,0:T(8,128)(2,1)}), bf16[1,512,2048]{2,1,0:T(8,128)(2,1)}) %all-gather.2.cloned.1.call-update) | async-done | bytes 2097168 | tf_op jit(solution)/shard_map/all_gather | solution.py:94
  121.0 2.1 fusion.5
  123.0 129.6 %all-to-all-done = bf16[32,64,2304]{2,1,0:T(8,128)(2,1)} async-done(((bf16[32,64,2304]{2,1,0:T(8,128)(2,1)}), bf16[32,64,2304]{2,1,0:T(8,128)(2,1)}, u32[]{:S(2)}, u32[]{:S(2)}) %all-to-all-start) | async-done | bytes 9437216 | tf_op jit(solution)/shard_map/all_to_all | solution.py:85
  252.7 1.4 slice_bitcast_fusion
  254.1 1.4 copy.35
  255.6 2.1 fusion.23
  259.9 3.2 fusion.10
  263.2 136.6 %all-reduce.2.cloned.1.call-done = bf16[1,512,2048]{2,1,0:T(8,128)(2,1)} async-done(((bf16[1,512,2048]{2,1,0:T(8,128)(2,1)}), bf16[1,512,2048]{2,1,0:T(8,128)(2,1)}) %all-reduce.2.cloned.1.call-update) | async-done | bytes 2097168 | tf_op jit(solution)/shard_map/psum | solution.py:114
  399.8 2.6 fusion.2
  402.4 6.2 %fusion = f32[512,1280]{1,0:T(8,128)S(1)} fusion(bf16[2048,2304]{1,0:T(8,128)(2,1)} %bitcast.7, bf16[1,512,2048]{2,1,0:T(8,128)(2,1)S(1)} %get-tuple-element.3, f32[2048]{0:T(1024)S(1)} %copy-done.9, f32[512]{0:T(512)S(1)} %add_rsqrt_fusion.1), kind=kOutput, calls=%fused_computation.7 | convolution fusion | flops 2688548864 | bytes 9971712 | tf_op jit(solution)/shard_map/dot_general | solution.py:118
  408.5 5.0 fusion.9
  415.2 0.8 scatter_fusion
  416.7 5.9 %all-to-all-start.1 = ((bf16[2,4,128,128]{3,2,0,1:T(8,128)(2,1)}), bf16[2,4,128,128]{3,2,0,1:T(8,128)(2,1)S(1)}, u32[]{:S(2)}, u32[]{:S(2)}) async-start(bf16[2,4,128,128]{3,2,0,1:T(8,128)(2,1)} %copy.38), calls=%async_computation.2 | async-start | bytes 524288 | tf_op jit(solution)/shard_map/all_to_all | solution.py:149
  422.7 6.7 %all-to-all-done.1 = bf16[2,4,128,128]{3,2,0,1:T(8,128)(2,1)S(1)} async-done(((bf16[2,4,128,128]{3,2,0,1:T(8,128)(2,1)}), bf16[2,4,128,128]{3,2,0,1:T(8,128)(2,1)S(1)}, u32[]{:S(2)}, u32[]{:S(2)}) %all-to-all-start.1) | async-done | bytes 262176 | tf_op jit(solution)/shard_map/all_to_all | solution.py:149
  429.5 0.8 scatter_fusion.1
  430.3 80.5 %reduce-scatter.2.cloned.1.call-done = bf16[1,512,256]{2,1,0:T(8,128)(2,1)} async-done(((bf16[1,512,2048]{2,1,0:T(8,128)(2,1)}), bf16[1,512,256]{2,1,0:T(8,128)(2,1)}) %reduce-scatter.2.cloned.1.call-update) | async-done | bytes 262160 | tf_op jit(solution)/shard_map/reduce_scatter | solution.py:121
  510.8 1.8 add_convert_fusion
  (66 shorter events, 6.5 us)
Async XLA Ops:
  7.2 0.9 copy-start
  16.5 236.1 %all-to-all-start = ((bf16[32,64,2304]{2,1,0:T(8,128)(2,1)}), bf16[32,64,2304]{2,1,0:T(8,128)(2,1)}, u32[]{:S(2)}, u32[]{:S(2)}) async-start(bf16[32,64,2304]{2,1,0:T(8,128)(2,1)} %stack.4), calls=%async_computation | async-start | bytes 18874368 | tf_op jit(solution)/shard_map/all_to_all | solution.py:85
  25.7 95.2 %all-gather.2.cloned.1.call-start = ((), (), s32[]{:S(2)}) async-start(), calls=%async_computation.3 | async-start | bytes 2359296 | tf_op jit(solution)/shard_map/all_gather | solution.py:94
  26.5 373.3 %all-reduce.2.cloned.1.call-start = ((), (), s32[]{:S(2)}) async-start(), calls=%async_computation.4 | async-start | bytes 4194304 | tf_op jit(solution)/shard_map/psum | solution.py:114
  252.7 2.9 copy-start.1
  255.5 2.3 copy-start.7
  255.6 2.7 copy-start.8
  255.6 2.8 copy-start.4
  255.6 2.8 copy-start.5
  263.1 139.3 %copy-start.9 = (f32[2048]{0:T(1024)S(1)}, f32[2048]{0:T(1024)}, u32[]{:S(2)}) copy-start(f32[2048]{0:T(1024)} %param.21) | copy-start | bytes 24580
  263.1 247.7 %reduce-scatter.2.cloned.1.call-start = ((), (), s32[]{:S(2)}) async-start(), calls=%async_computation.5 | async-start | bytes 2359296 | tf_op jit(solution)/shard_map/reduce_scatter | solution.py:121
  402.3 6.2 %copy-start.2 = (bf16[1,512,2048]{2,1,0:T(8,128)(2,1)}, bf16[1,512,2048]{2,1,0:T(8,128)(2,1)S(1)}, u32[]{:S(2)}) copy-start(bf16[1,512,2048]{2,1,0:T(8,128)(2,1)S(1)} %get-tuple-element.3) | copy-start | bytes 6291460
  413.6 0.7 copy-start.6
  416.7 12.8 %all-to-all-start.1 = ((bf16[2,4,128,128]{3,2,0,1:T(8,128)(2,1)}), bf16[2,4,128,128]{3,2,0,1:T(8,128)(2,1)S(1)}, u32[]{:S(2)}, u32[]{:S(2)}) async-start(bf16[2,4,128,128]{3,2,0,1:T(8,128)(2,1)} %copy.38), calls=%async_computation.2 | async-start | bytes 524288 | tf_op jit(solution)/shard_map/all_to_all | solution.py:149
  430.3 82.3 %copy-start.3 = (bf16[2,4,128,128]{3,2,1,0:T(8,128)(2,1)}, bf16[2,4,128,128]{3,2,1,0:T(8,128)(2,1)S(1)}, u32[]{:S(2)}) copy-start(bf16[2,4,128,128]{3,2,1,0:T(8,128)(2,1)S(1)} %scatter_fusion.1) | copy-start | bytes 786436
Sparse Core Ops, SparseCore 0:
  29.0 91.9 all-gather.1
  263.2 136.4 all-reduce.1
  413.7 97.0 reduce-scatter.1
